TPU v7x, 512 devices: a whole 4x8x8 slice. The times are simulated.
512 devices in a mesh: sub: 128 (over z, y, core), harm: 4 (over x).
Axes of the slice: x: 4, y: 8, z: 8, core: 2. Of those that a mesh axis runs over, the one named last changes fastest.
Arguments:
- lengths: int32 [384], P('sub'), may hold values from 128 to 1024, as said below
- owners: int32 [384, 1], P('sub'), may hold values from 0 to 127, as said below
- front_inverse: bfloat16 [384, 1024, 1024], P('sub', 'harm'), may hold values from -0.1875 to 0.1875
- coupling: bfloat16 [384, 1024, 768], P('sub', 'harm'), may hold values from -0.1875 to 0.1875
- stiffness: bfloat16 [384, 768, 768], P('sub', 'harm'), may hold values from -0.21875 to 0.21875
- displacement: bfloat16 [128, 32, 768], P('sub', 'harm'), may hold values from -6 to 6
- forcing: float32 [128, 32, 768], P('sub', 'harm'), may hold values from -6 to 6
- lumped_mass: float32 [128, 768], P('sub'), may hold values from 0.2 to 2
- damping: float32 [128, 768], P('sub'), may hold values from 0.1 to 1.5
Outputs:
- interior: bfloat16 [384, 32, 1024], P('sub', None, 'harm')
- residual: float32 [128, 32, 768], P('sub', 'harm')
- modes: bfloat16 [384, 1024, 768], P('sub', 'harm')
Inputs may be any that keep to these rules, and one draw needn't show every extreme that they name: `lengths`: live interior front rows of each substructure, which are its first rows; some substructure has all 1024. `owners`: substructure k lies on sub index k // 3; on every sub index d, the first 2 of its 3 substructures are attached to block (d + 64) mod 128, the third to a block of uneven popularity; every interface block has at least one substructure.
All inputs are finite; a program needn't handle non-finite values.
Results may differ from a plain program's by a relative error of at most 0.008.
Values may be sent and summed in bfloat16 or wider, within the bound.
No kernel may reach another device: no remote copies, remote signals or barrier semaphores. Data moves between devices by JAX's collectives and lax.ppermute only.
A program may use at most 64 MiB of HBM per device.

v0:
```python
import jax
import jax.numpy as jnp
from jax import lax
from jax.sharding import Mesh
from jax.sharding import PartitionSpec as P

SUB = ("sub_0", "sub_1", "sub_2")
PLANE = ("sub_0", "sub_1")
PAIR = ("sub_2", "harm")


def copy_for_each(x, axis):
    length = lax.axis_size(axis)
    return lax.all_to_all(jnp.broadcast_to(x[None], (length, *x.shape)), axis, 0, 0, tiled=True)


def joined_along(tiles, dim):
    tiles = jnp.moveaxis(tiles, 0, dim)
    shape = tiles.shape
    return tiles.reshape(*shape[:dim], shape[dim] * shape[dim + 1], *shape[dim + 2 :])


def whole_of(x, axes, dim):
    far, near = axes
    tiles = copy_for_each(copy_for_each(x, far), near)
    return joined_along(tiles.swapaxes(0, 1).reshape(-1, *x.shape), dim)


def collect(x, axis, dim):
    tiles = copy_for_each(x, axis)
    return joined_along(tiles, dim)


def in_blocks(x, dim, length):
    shape = x.shape
    tiles = x.reshape(*shape[:dim], length, shape[dim] // length, *shape[dim + 1 :])
    return jnp.moveaxis(tiles, dim, 0)


def sent_and_summed(x, axis, dim):
    tiles = in_blocks(x, dim, lax.axis_size(axis))
    arrived = lax.all_to_all(tiles, axis, split_axis=0, concat_axis=0, tiled=True)
    return arrived.astype(jnp.float32).sum(axis=0)


def body(
    lengths, owners, front_inverse, coupling, stiffness, displacement, forcing, lumped_mass, damping
):
    nharm = lax.axis_size("harm")
    harm_idx = lax.axis_index("harm")
    front_q = coupling.shape[1]
    width = coupling.shape[2]
    width_q = stiffness.shape[1]
    nown = lax.axis_size(SUB)
    own_rows = harm_idx * front_q + jnp.arange(front_q, dtype=jnp.int32)
    live_rows = own_rows[None, :] < lengths[:, None]
    masked = jnp.where(live_rows[:, :, None], coupling, jnp.zeros_like(coupling))
    piece = lax.all_gather(coupling, "harm", axis=1, tiled=True)
    live_cols = jnp.arange(nharm * front_q, dtype=jnp.int32)[None, :] < lengths[:, None]
    front_live = jnp.where(live_cols[:, None, :], front_inverse, jnp.zeros_like(front_inverse))
    modes = jnp.einsum(
        "sfg,sgn->sfn", front_live, piece, preferred_element_type=jnp.float32
    ).astype(jnp.bfloat16)
    nplane = lax.axis_size(PLANE)
    rows_q = displacement.shape[1]
    core = lax.axis_index("sub_2")
    near = (lax.axis_index(SUB) + nown // 2) % nown
    third = owners[2, 0]
    other = lax.ppermute(owners[2:3, 0], "sub_2", [(0, 1), (1, 0)])[0]
    plane = copy_for_each(displacement[0], PLANE)
    lent = lax.ppermute(
        lax.dynamic_index_in_dim(plane, other // 2, 0, keepdims=False), "sub_2", [(0, 1), (1, 0)]
    )
    here = lax.dynamic_index_in_dim(plane, third // 2, 0, keepdims=False)
    picked = jnp.stack(
        [
            lax.dynamic_index_in_dim(plane, near // 2, 0, keepdims=False),
            jnp.where(third % 2 == core, here, lent),
        ]
    )
    own_pair = collect(picked, "harm", 1)
    own_disp = jnp.stack([own_pair[0], own_pair[0], own_pair[1]])
    inner = -jnp.einsum("sfn,shn->shf", modes, own_disp, preferred_element_type=jnp.float32)
    interior = jnp.where(live_rows[:, None, :], inner, jnp.float32(0.0)).astype(jnp.bfloat16)
    disp_cols = lax.dynamic_slice_in_dim(own_disp, harm_idx * width_q, width_q, 2)
    contrib = jnp.einsum("shf,sfn->shn", interior, masked, preferred_element_type=jnp.float32)
    contrib = contrib + jnp.einsum(
        "shj,sjn->shn", disp_cols, stiffness, preferred_element_type=jnp.float32
    )
    near_c = (contrib[0] + contrib[1]).reshape(nharm, rows_q, width)
    third_c = contrib[2].reshape(nharm, rows_q, width)
    zero_rows = jnp.zeros_like(near_c)
    send = jnp.stack(
        [
            jnp.stack(
                [
                    jnp.where(peer_core == core, near_c, zero_rows),
                    jnp.where(third % 2 == peer_core, third_c, zero_rows),
                ],
                axis=1,
            )
            for peer_core in range(2)
        ]
    )
    came = lax.all_to_all(
        send.reshape(2 * nharm, 2, rows_q, width).astype(jnp.bfloat16), PAIR, 0, 0, tiled=True
    ).astype(jnp.float32)
    came = came.reshape(2, nharm, 2, rows_q, width).sum(axis=1)
    mine = jnp.where(core == 0, came[0], came[1])
    theirs = jnp.where(core == 0, came[1], came[0])
    near_part = mine[0]
    third_part = mine[1]
    other_part = theirs[1]
    slots = jnp.arange(nplane, dtype=jnp.int32)[:, None, None]
    dense = (
        jnp.where(slots == near // 2, near_part, jnp.float32(0.0))
        + jnp.where((slots == third // 2) & (third % 2 == core), third_part, jnp.float32(0.0))
        + jnp.where((slots == other // 2) & (other % 2 == core), other_part, jnp.float32(0.0))
    )
    arrived = lax.all_to_all(
        dense.astype(jnp.bfloat16), PLANE, split_axis=0, concat_axis=0, tiled=True
    ).astype(jnp.float32)
    gathered = jnp.sum(arrived, axis=0, keepdims=True)
    rows_q = displacement.shape[1]
    pairs_all = rows_q * nharm // 2
    rows = harm_idx * rows_q + jnp.arange(rows_q, dtype=jnp.int32)
    pair = (rows // 2).astype(jnp.float32)
    parity = (rows % 2).astype(jnp.float32)
    freq = 1.5 * (pair + 1.0) / pairs_all
    sign = 1.0 - 2.0 * parity
    disp = displacement.astype(jnp.float32)
    partner = disp.reshape(1, rows_q // 2, 2, width)[:, :, ::-1, :].reshape(1, rows_q, width)
    residual = (
        gathered
        - (freq * freq)[None, :, None] * lumped_mass[:, None, :] * disp
        + (sign * freq)[None, :, None] * damping[:, None, :] * partner
        - forcing
    )
    return (interior, residual, modes)


def solution(mesh):
    split = Mesh(
        mesh.devices.reshape(8, 8, 2, mesh.shape["harm"]), ("sub_0", "sub_1", "sub_2", "harm")
    )
    placed = (
        P(SUB),
        P(SUB, None),
        P(SUB, "harm", None),
        P(SUB, "harm", None),
        P(SUB, "harm", None),
        P(SUB, "harm", None),
        P(SUB, "harm", None),
        P(SUB, None),
        P(SUB, None),
    )
    return jax.shard_map(
        body,
        mesh=split,
        in_specs=placed,
        out_specs=(P(SUB, None, "harm"), P(SUB, "harm", None), P(SUB, "harm", None)),
        check_vma=False,
    )
```

profile of v0, /device:TPU:8, one launch (start us, length us, event | category | flops | bytes accessed | tf_op | source)
XLA Modules:
  0.0 136.1 jit_solution(10824814379573062923)
XLA Ops:
  7.2 0.7 all-gather.2.cloned.1.call-update
  7.9 1.6 %broadcast_in_dim.101 = bf16[64,8,768]{2,1,0:T(8,128)(2,1)} broadcast(bf16[8,768]{1,0:T(8,128)(2,1)} %bitcast.58), dimensions={1,2} | broadcast | bytes 798720 | tf_op jit(solution)/shard_map/broadcast_in_dim | solution.py:14
  9.6 16.6 %all-to-all-start = ((bf16[64,8,768]{2,1,0:T(8,128)(2,1)}), bf16[64,8,768]{2,1,0:T(8,128)(2,1)S(1)}, u32[]{:S(2)}, u32[]{:S(2)}) async-start(bf16[64,8,768]{2,1,0:T(8,128)(2,1)} %broadcast_in_dim.101), calls=%async_computation | async-start | bytes 1572864 | tf_op jit(solution)/shard_map/all_to_all | solution.py:14
  26.2 0.6 slice.46
  26.8 1.9 %collective-permute-start = (s32[1]{0:T(128)}, s32[1]{0:T(128)}, u32[]{:S(2)}, u32[]{:S(2)}) collective-permute-start(s32[1]{0:T(128)} %bitcast.3), channel_id=1, source_target_pairs={{0,4},{4,0},{1,5},{5,1},{2,6},{6,2},{3,7},{7,3},{8,12},{12,8},{9,1... | collective-permute-start | bytes 20 | tf_op jit(solution)/shard_map/ppermute | solution.py:69
  28.8 1.1 collective-permute-done
  32.4 17.7 %all-to-all-done = bf16[64,8,768]{2,1,0:T(8,128)(2,1)S(1)} async-done(((bf16[64,8,768]{2,1,0:T(8,128)(2,1)}), bf16[64,8,768]{2,1,0:T(8,128)(2,1)S(1)}, u32[]{:S(2)}, u32[]{:S(2)}) %all-to-all-start) | async-done | bytes 786464 | tf_op jit(solution)/shard_map/all_to_all | solution.py:14
  50.1 1.9 %collective-permute-start.1 = (bf16[8,768]{1,0:T(8,128)(2,1)S(1)}, bf16[8,768]{1,0:T(8,128)(2,1)S(1)}, u32[]{:S(2)}, u32[]{:S(2)}) collective-permute-start(bf16[8,768]{1,0:T(8,128)(2,1)S(1)} %get-tuple-element.4), channel_id=1, source_target_pairs={{0,4},{4,0},{1,5},{5,1},{2,6},{6,2},{3,7},{7,3},{8,12},{12,8},{9,1... | collective-permute-start | bytes 36872 | tf_op jit(solution)/shard_map/ppermute | solution.py:71
  54.7 0.6 broadcast_in_dim.102
  55.4 4.3 %all-to-all-start.1 = ((bf16[4,2,8,768]{3,2,1,0:T(8,128)(2,1)}), bf16[4,2,8,768]{3,2,1,0:T(8,128)(2,1)S(1)}, u32[]{:S(2)}, u32[]{:S(2)}) async-start(bf16[4,2,8,768]{3,2,1,0:T(8,128)(2,1)} %broadcast_in_dim.102), calls=%async_computation.1 | async-start | bytes 196608 | tf_op jit(solution)/shard_map/all_to_all | solution.py:14
  59.7 7.0 %all-to-all-done.1 = bf16[4,2,8,768]{3,2,1,0:T(8,128)(2,1)S(1)} async-done(((bf16[4,2,8,768]{3,2,1,0:T(8,128)(2,1)}), bf16[4,2,8,768]{3,2,1,0:T(8,128)(2,1)S(1)}, u32[]{:S(2)}, u32[]{:S(2)}) %all-to-all-start.1) | async-done | bytes 98336 | tf_op jit(solution)/shard_map/all_to_all | solution.py:14
  66.8 1.1 fusion.20
  67.9 5.9 %all-gather.2.cloned.1.call-done = bf16[3,1024,768]{2,1,0:T(8,128)(2,1)} async-done(((bf16[3,256,768]{2,1,0:T(8,128)(2,1)}), bf16[3,1024,768]{2,1,0:T(8,128)(2,1)}) %all-gather.2.cloned.1.call-update) | async-done | bytes 4718608 | tf_op jit(solution)/shard_map/all_gather | solution.py:58
  73.7 4.2 %fusion.3 = bf16[3,256,768]{2,1,0:T(8,128)(2,1)S(1)} fusion(bf16[3,1024,768]{2,1,0:T(8,128)(2,1)} %all-gather.2.cloned.1.call-done, bf16[3,256,1024]{2,1,0:T(8,128)(2,1)} %param.11, pred[3,1024]{1,0:T(4,128)(4,1)S(1)} %iota_compare_fusion), kind=kOutput, calls=%fused_computation.5 | convolution fusion | flops 1209335808 | bytes 7474176 | tf_op jit(solution)/shard_map/sfg,sgn->sfn/dot_general | solution.py:61
  78.0 0.5 fusion.13
  78.5 0.4 fusion.9
  79.1 0.7 pad_maximum_fusion
  79.8 3.4 %all-to-all-start.2 = ((bf16[8,2,8,768]{3,2,1,0:T(8,128)(2,1)}), bf16[8,2,8,768]{3,2,1,0:T(8,128)(2,1)S(1)}, u32[]{:S(2)}, u32[]{:S(2)}) async-start(bf16[8,2,8,768]{3,2,1,0:T(8,128)(2,1)} %bitcast.20), calls=%async_computation.2 | async-start | bytes 393216 | tf_op jit(solution)/shard_map/all_to_all | solution.py:105
  83.2 6.2 %all-to-all-done.2 = bf16[8,2,8,768]{3,2,1,0:T(8,128)(2,1)S(1)} async-done(((bf16[8,2,8,768]{3,2,1,0:T(8,128)(2,1)}), bf16[8,2,8,768]{3,2,1,0:T(8,128)(2,1)S(1)}, u32[]{:S(2)}, u32[]{:S(2)}) %all-to-all-start.2) | async-done | bytes 196640 | tf_op jit(solution)/shard_map/all_to_all | solution.py:105
  89.6 1.3 add_convert_fusion
  90.8 13.4 %all-to-all-start.3 = ((bf16[64,8,768]{2,1,0:T(8,128)(2,1)}), bf16[64,8,768]{2,1,0:T(8,128)(2,1)S(1)}, u32[]{:S(2)}, u32[]{:S(2)}) async-start(bf16[64,8,768]{2,1,0:T(8,128)(2,1)} %add_convert_fusion), calls=%async_computation.3 | async-start | bytes 1572864 | tf_op jit(solution)/shard_map/all_to_all | solution.py:120
  104.2 0.2 rev.3
  104.6 23.9 %all-to-all-done.3 = bf16[64,8,768]{2,1,0:T(8,128)(2,1)S(1)} async-done(((bf16[64,8,768]{2,1,0:T(8,128)(2,1)}), bf16[64,8,768]{2,1,0:T(8,128)(2,1)S(1)}, u32[]{:S(2)}, u32[]{:S(2)}) %all-to-all-start.3) | async-done | bytes 786464 | tf_op jit(solution)/shard_map/all_to_all | solution.py:120
  128.6 0.7 fusion.24
  (47 shorter events, 0.7 us)
Async XLA Ops:
  7.2 59.6 %copy-start = (bf16[3,192,768]{2,1,0:T(8,128)(2,1)S(1)}, bf16[3,192,768]{2,1,0:T(8,128)(2,1)}, u32[]{:S(2)}) copy-start(bf16[3,192,768]{2,1,0:T(8,128)(2,1)} %param.13) | copy-start | bytes 2654212
  7.2 19.0 %copy-start.10 = (s32[3,1]{0,1:T(1,128)S(1)}, s32[3,1]{0,1:T(1,128)}, u32[]{:S(2)}) copy-start(s32[3,1]{0,1:T(1,128)} %param.10) | copy-start | bytes 40
  7.2 21.5 %copy-start.9 = (s32[3]{0:T(128)S(1)}, s32[3]{0:T(128)}, u32[]{:S(2)}) copy-start(s32[3]{0:T(128)} %param.9) | copy-start | bytes 40
  7.2 66.5 %all-gather.2.cloned.1.call-start = ((), (), s32[]{:S(2)}) async-start(), calls=%async_computation.4 | async-start | bytes 5898240 | tf_op jit(solution)/shard_map/all_gather | solution.py:58
  9.6 40.6 %all-to-all-start = ((bf16[64,8,768]{2,1,0:T(8,128)(2,1)}), bf16[64,8,768]{2,1,0:T(8,128)(2,1)S(1)}, u32[]{:S(2)}, u32[]{:S(2)}) async-start(bf16[64,8,768]{2,1,0:T(8,128)(2,1)} %broadcast_in_dim.101), calls=%async_computation | async-start | bytes 1572864 | tf_op jit(solution)/shard_map/all_to_all | solution.py:14
  26.8 3.1 %collective-permute-start = (s32[1]{0:T(128)}, s32[1]{0:T(128)}, u32[]{:S(2)}, u32[]{:S(2)}) collective-permute-start(s32[1]{0:T(128)} %bitcast.3), channel_id=1, source_target_pairs={{0,4},{4,0},{1,5},{5,1},{2,6},{6,2},{3,7},{7,3},{8,12},{12,8},{9,1... | collective-permute-start | bytes 20 | tf_op jit(solution)/shard_map/ppermute | solution.py:69
  50.1 4.6 %collective-permute-start.1 = (bf16[8,768]{1,0:T(8,128)(2,1)S(1)}, bf16[8,768]{1,0:T(8,128)(2,1)S(1)}, u32[]{:S(2)}, u32[]{:S(2)}) collective-permute-start(bf16[8,768]{1,0:T(8,128)(2,1)S(1)} %get-tuple-element.4), channel_id=1, source_target_pairs={{0,4},{4,0},{1,5},{5,1},{2,6},{6,2},{3,7},{7,3},{8,12},{12,8},{9,1... | collective-permute-start | bytes 36872 | tf_op jit(solution)/shard_map/ppermute | solution.py:71
  55.4 11.4 %all-to-all-start.1 = ((bf16[4,2,8,768]{3,2,1,0:T(8,128)(2,1)}), bf16[4,2,8,768]{3,2,1,0:T(8,128)(2,1)S(1)}, u32[]{:S(2)}, u32[]{:S(2)}) async-start(bf16[4,2,8,768]{3,2,1,0:T(8,128)(2,1)} %broadcast_in_dim.102), calls=%async_computation.1 | async-start | bytes 196608 | tf_op jit(solution)/shard_map/all_to_all | solution.py:14
  67.9 10.6 %copy-start.1 = (bf16[3,256,768]{2,1,0:T(8,128)(2,1)S(1)}, bf16[3,256,768]{2,1,0:T(8,128)(2,1)}, u32[]{:S(2)}) copy-start(bf16[3,256,768]{2,1,0:T(8,128)(2,1)} %param.12) | copy-start | bytes 3538948
  73.7 4.8 %copy-start.3 = (f32[3,32,768]{2,1,0:T(8,128)S(1)}, f32[3,32,768]{2,1,0:T(8,128)}, u32[]{:S(2)}) copy-start(f32[3,32,768]{2,1,0:T(8,128)} %fusion.20) | copy-start | bytes 884740
  78.0 1.0 copy-start.2
  78.5 1.3 copy-start.5
  79.8 9.7 %all-to-all-start.2 = ((bf16[8,2,8,768]{3,2,1,0:T(8,128)(2,1)}), bf16[8,2,8,768]{3,2,1,0:T(8,128)(2,1)S(1)}, u32[]{:S(2)}, u32[]{:S(2)}) async-start(bf16[8,2,8,768]{3,2,1,0:T(8,128)(2,1)} %bitcast.20), calls=%async_computation.2 | async-start | bytes 393216 | tf_op jit(solution)/shard_map/all_to_all | solution.py:105
  83.2 21.0 %copy-start.4 = (bf16[1,8,768]{2,1,0:T(8,128)(2,1)S(1)}, bf16[1,8,768]{2,1,0:T(8,128)(2,1)}, u32[]{:S(2)}) copy-start(bf16[1,8,768]{2,1,0:T(8,128)(2,1)} %param.14) | copy-start | bytes 36868
  89.5 15.0 %copy-start.7 = (f32[1,768]{1,0:T(1,128)S(1)}, f32[1,768]{1,0:T(1,128)}, u32[]{:S(2)}) copy-start(f32[1,768]{1,0:T(1,128)} %param.17) | copy-start | bytes 9220
  89.5 15.0 %copy-start.8 = (f32[1,768]{1,0:T(1,128)S(1)}, f32[1,768]{1,0:T(1,128)}, u32[]{:S(2)}) copy-start(f32[1,768]{1,0:T(1,128)} %param.16) | copy-start | bytes 9220
  89.6 39.0 %copy-start.6 = (f32[1,8,768]{2,1,0:T(8,128)S(1)}, f32[1,8,768]{2,1,0:T(8,128)}, u32[]{:S(2)}) copy-start(f32[1,8,768]{2,1,0:T(8,128)} %param.15) | copy-start | bytes 73732
  90.8 37.6 %all-to-all-start.3 = ((bf16[64,8,768]{2,1,0:T(8,128)(2,1)}), bf16[64,8,768]{2,1,0:T(8,128)(2,1)S(1)}, u32[]{:S(2)}, u32[]{:S(2)}) async-start(bf16[64,8,768]{2,1,0:T(8,128)(2,1)} %add_convert_fusion), calls=%async_computation.3 | async-start | bytes 1572864 | tf_op jit(solution)/shard_map/all_to_all | solution.py:120
Sparse Core Ops, SparseCore 0:
  10.1 63.5 all-gather.1
where the time goes:
time: 137 us; the launch traced here: 136 us
  waiting for transfers between devices  62.5 us (46%)
  starting transfers between devices  41.5 us (30%)
  between operations  19.6 us (14%)
  matrix products  6.18 us (5%)
  local copies, waits for them, and re-layouts  3.31 us (2%)
  other arithmetic  3.12 us (2%)
    all_to_all x2, waiting for transfers between devices, copy_for_each(): lax.all_to_all(jnp.broadcast_to(x[None], (length, *x.shape)), axis, 0, 0,...  24.7 us
    all_to_all x1, waiting for transfers between devices, body(): lax.all_to_all(dense.astype(jnp.bfloat16), PLANE, split_axis=0, concat_ax...  23.9 us
    all_to_all x2, starting transfers between devices, copy_for_each(): lax.all_to_all(jnp.broadcast_to(x[None], (length, *x.shape)), axis, 0, 0,...  20.9 us
    all_to_all x1, starting transfers between devices, body(): lax.all_to_all(dense.astype(jnp.bfloat16), PLANE, split_axis=0, concat_ax...  13.4 us
    all_to_all x1, waiting for transfers between devices, body(): lax.all_to_all(send.reshape(2 * nharm, 2, rows_q, width).astype(jnp.bfloa...  6.23 us
    all_gather x1, waiting for transfers between devices, body(): piece = lax.all_gather(coupling, 'harm', axis=1, tiled=True)  5.86 us
    dot_general x1, matrix products, body(): jnp.einsum('sfg,sgn->sfn', front_live, piece, preferred_element_type=jnp....  4.24 us
    all_to_all x1, starting transfers between devices, body(): lax.all_to_all(send.reshape(2 * nharm, 2, rows_q, width).astype(jnp.bfloa...  3.42 us
  transfers between devices with their start and end apart: 7, of which 6 were waited for; matrix products, arithmetic and copies ran while one was open for 3% of the time, Pallas kernels for 0%

commit v1 on v0

--- a/solution.py
+++ b/solution.py
@@ -55,7 +55,8 @@
     own_rows = harm_idx * front_q + jnp.arange(front_q, dtype=jnp.int32)
     live_rows = own_rows[None, :] < lengths[:, None]
     masked = jnp.where(live_rows[:, :, None], coupling, jnp.zeros_like(coupling))
-    piece = lax.all_gather(coupling, "harm", axis=1, tiled=True)
+    sent = jnp.stack([coupling] * lax.axis_size("harm"))
+    piece = jnp.concatenate(lax.all_to_all(sent, "harm", 0, 0), axis=1)
     live_cols = jnp.arange(nharm * front_q, dtype=jnp.int32)[None, :] < lengths[:, None]
     front_live = jnp.where(live_cols[:, None, :], front_inverse, jnp.zeros_like(front_inverse))
     modes = jnp.einsum(

time: 137 us -> 168 us (1.23)
  waiting for transfers between devices: 62.5 us -> 102 us
  between operations: 19.6 us -> 6.46 us
  blocking collectives: 0 us -> 9.89 us
  starting transfers between devices: 41.5 us -> 35.5 us
  local copies, waits for them, and re-layouts: 3.31 us -> 8.24 us
  matrix products: 6.18 us -> 2.62 us
    all_to_all x0 -> x1, waiting for transfers between devices: none -> 53.4 us  [body(): piece = jnp.concatenate(lax.all_to_all(sent, 'harm', 0, 0), axis=1)]
    all_to_all x0 -> x1, blocking collectives: none -> 9.89 us  [copy_for_each(): lax.all_to_all(jnp.broadcast_to(x[None], (length, *x.shape)), axis, 0, 0,...]
    all_to_all x2 -> x1, waiting for transfers between devices: 24.7 us -> 17.5 us  [copy_for_each(): lax.all_to_all(jnp.broadcast_to(x[None], (length, *x.shape)), axis, 0, 0,...]
    all_to_all x1, starting transfers between devices: 13.4 us -> 6.56 us  [body(): lax.all_to_all(dense.astype(jnp.bfloat16), PLANE, split_axis=0, concat_ax...]
    all_gather x1 -> x0, waiting for transfers between devices: 5.86 us -> none  [body(): piece = lax.all_gather(coupling, 'harm', axis=1, tiled=True)]
    all_to_all x0 -> x1, starting transfers between devices: none -> 5.1 us  [body(): piece = jnp.concatenate(lax.all_to_all(sent, 'harm', 0, 0), axis=1)]
    all_to_all x2 -> x1, starting transfers between devices: 20.9 us -> 16.6 us  [copy_for_each(): lax.all_to_all(jnp.broadcast_to(x[None], (length, *x.shape)), axis, 0, 0,...]
    dot_general x1, matrix products: 4.24 us -> 1.39 us  [body(): jnp.einsum('sfg,sgn->sfn', front_live, piece, preferred_element_type=jnp....]
  transfers between devices with their start and end apart: 7 -> 6, of which waited for: 6 -> 5; matrix products, arithmetic and copies ran while one was open for 3% -> 1% of each run, Pallas kernels for 0% -> 0%
where the time goes in v1:
time: 168 us
  waiting for transfers between devices  102 us (61%)
  starting transfers between devices  35.5 us (21%)
  blocking collectives  9.89 us (6%)
  local copies, waits for them, and re-layouts  8.24 us (5%)
  between operations  6.46 us (4%)
  other arithmetic  3.13 us (2%)
  matrix products  2.62 us (2%)
    all_to_all x1, waiting for transfers between devices, body(): piece = jnp.concatenate(lax.all_to_all(sent, 'harm', 0, 0), axis=1)  53.4 us
    all_to_all x1, waiting for transfers between devices, body(): lax.all_to_all(dense.astype(jnp.bfloat16), PLANE, split_axis=0, concat_ax...  23.9 us
    all_to_all x1, waiting for transfers between devices, copy_for_each(): lax.all_to_all(jnp.broadcast_to(x[None], (length, *x.shape)), axis, 0, 0,...  17.5 us
    all_to_all x1, starting transfers between devices, copy_for_each(): lax.all_to_all(jnp.broadcast_to(x[None], (length, *x.shape)), axis, 0, 0,...  16.6 us
    all_to_all x1, blocking collectives, copy_for_each(): lax.all_to_all(jnp.broadcast_to(x[None], (length, *x.shape)), axis, 0, 0,...  9.89 us
    all_to_all x1, starting transfers between devices, body(): lax.all_to_all(dense.astype(jnp.bfloat16), PLANE, split_axis=0, concat_ax...  6.56 us
    all_to_all x1, waiting for transfers between devices, body(): lax.all_to_all(send.reshape(2 * nharm, 2, rows_q, width).astype(jnp.bfloa...  6.15 us
    all_to_all x1, starting transfers between devices, body(): piece = jnp.concatenate(lax.all_to_all(sent, 'harm', 0, 0), axis=1)  5.1 us
  transfers between devices with their start and end apart: 6, of which 5 were waited for; matrix products, arithmetic and copies ran while one was open for 1% of the time, Pallas kernels for 0%

profile of v1, /device:TPU:8, one launch (start us, length us, event | category | flops | bytes accessed | tf_op | source)
XLA Modules:
  0.0 167.8 jit_solution(13931360056682022554)
XLA Ops:
  0.7 1.8 %broadcast_in_dim.101 = bf16[64,8,768]{2,1,0:T(8,128)(2,1)} broadcast(bf16[8,768]{1,0:T(8,128)(2,1)} %bitcast.61), dimensions={1,2} | broadcast | bytes 798720 | tf_op jit(solution)/shard_map/broadcast_in_dim | solution.py:14
  2.4 16.6 %all-to-all-start = ((bf16[64,8,768]{2,1,0:T(8,128)(2,1)}), bf16[64,8,768]{2,1,0:T(8,128)(2,1)S(1)}, u32[]{:S(2)}, u32[]{:S(2)}) async-start(bf16[64,8,768]{2,1,0:T(8,128)(2,1)} %broadcast_in_dim.101), calls=%async_computation | async-start | bytes 1572864 | tf_op jit(solution)/shard_map/all_to_all | solution.py:14
  19.0 0.6 slice.46
  19.6 1.9 %collective-permute-start = (s32[1]{0:T(128)}, s32[1]{0:T(128)}, u32[]{:S(2)}, u32[]{:S(2)}) collective-permute-start(s32[1]{0:T(128)} %bitcast.3), channel_id=1, source_target_pairs={{0,4},{4,0},{1,5},{5,1},{2,6},{6,2},{3,7},{7,3},{8,12},{12,8},{9,1... | collective-permute-start | bytes 20 | tf_op jit(solution)/shard_map/ppermute | solution.py:70
  21.6 1.2 collective-permute-done
  25.5 17.5 %all-to-all-done = bf16[64,8,768]{2,1,0:T(8,128)(2,1)S(1)} async-done(((bf16[64,8,768]{2,1,0:T(8,128)(2,1)}), bf16[64,8,768]{2,1,0:T(8,128)(2,1)S(1)}, u32[]{:S(2)}, u32[]{:S(2)}) %all-to-all-start) | async-done | bytes 786464 | tf_op jit(solution)/shard_map/all_to_all | solution.py:14
  43.0 1.9 %collective-permute-start.1 = (bf16[8,768]{1,0:T(8,128)(2,1)S(1)}, bf16[8,768]{1,0:T(8,128)(2,1)S(1)}, u32[]{:S(2)}, u32[]{:S(2)}) collective-permute-start(bf16[8,768]{1,0:T(8,128)(2,1)S(1)} %get-tuple-element.4), channel_id=1, source_target_pairs={{0,4},{4,0},{1,5},{5,1},{2,6},{6,2},{3,7},{7,3},{8,12},{12,8},{9,1... | collective-permute-start | bytes 36872 | tf_op jit(solution)/shard_map/ppermute | solution.py:72
  47.6 9.9 %all_to_all.25 = bf16[4,2,8,768]{3,2,1,0:T(8,128)(2,1)S(1)} all-to-all(bf16[4,2,8,768]{3,2,1,0:T(8,128)(2,1)S(1)} %broadcast_in_dim.102), channel_id=1, replica_groups=mesh['sub_0'=8,'sub_1'=8,'sub_2'=2,'harm'=4] {'harm'}, dimensions={0} | all-to-all | bytes 196608 | tf_op jit(solution)/shard_map/all_to_all | solution.py:14
  57.5 2.6 %stack.44 = bf16[4,3,256,768]{3,2,1,0:T(8,128)(2,1)} broadcast(bf16[3,256,768]{2,1,0:T(8,128)(2,1)S(1)} %copy-done.2), dimensions={1,2,3} | broadcast | bytes 5898240 | tf_op jit(solution)/shard_map/stack | solution.py:58
  60.1 5.1 %all-to-all-start.2 = ((bf16[4,3,256,768]{3,2,1,0:T(8,128)(2,1)}), bf16[4,3,256,768]{3,2,1,0:T(8,128)(2,1)}, u32[]{:S(2)}, u32[]{:S(2)}) async-start(bf16[4,3,256,768]{3,2,1,0:T(8,128)(2,1)} %stack.44), calls=%async_computation.2 | async-start | bytes 9437184 | tf_op jit(solution)/shard_map/all_to_all | solution.py:59
  65.4 0.3 fusion.20
  65.8 53.4 %all-to-all-done.2 = bf16[4,3,256,768]{3,2,1,0:T(8,128)(2,1)} async-done(((bf16[4,3,256,768]{3,2,1,0:T(8,128)(2,1)}), bf16[4,3,256,768]{3,2,1,0:T(8,128)(2,1)}, u32[]{:S(2)}, u32[]{:S(2)}) %all-to-all-start.2) | async-done | bytes 4718624 | tf_op jit(solution)/shard_map/all_to_all | solution.py:59
  119.2 2.8 %copy.21 = bf16[3,4,256,768]{3,2,1,0:T(8,128)(2,1)S(1)} copy(bf16[3,4,256,768]{3,2,0,1:T(8,128)(2,1)} %bitcast.10) | data formatting | bytes 9437184 | tf_op jit(solution)/shard_map/reshape | solution.py:59
  122.0 1.4 fusion.3
  123.4 0.5 fusion.13
  124.0 0.4 fusion.9
  124.5 0.7 pad_maximum_fusion
  125.2 3.4 %all-to-all-start.3 = ((bf16[8,2,8,768]{3,2,1,0:T(8,128)(2,1)}), bf16[8,2,8,768]{3,2,1,0:T(8,128)(2,1)S(1)}, u32[]{:S(2)}, u32[]{:S(2)}) async-start(bf16[8,2,8,768]{3,2,1,0:T(8,128)(2,1)} %bitcast.22), calls=%async_computation.3 | async-start | bytes 393216 | tf_op jit(solution)/shard_map/all_to_all | solution.py:106
  128.7 6.1 %all-to-all-done.3 = bf16[8,2,8,768]{3,2,1,0:T(8,128)(2,1)S(1)} async-done(((bf16[8,2,8,768]{3,2,1,0:T(8,128)(2,1)}), bf16[8,2,8,768]{3,2,1,0:T(8,128)(2,1)S(1)}, u32[]{:S(2)}, u32[]{:S(2)}) %all-to-all-start.3) | async-done | bytes 196640 | tf_op jit(solution)/shard_map/all_to_all | solution.py:106
  134.9 1.3 add_convert_fusion
  136.2 6.6 %all-to-all-start.4 = ((bf16[64,8,768]{2,1,0:T(8,128)(2,1)}), bf16[64,8,768]{2,1,0:T(8,128)(2,1)S(1)}, u32[]{:S(2)}, u32[]{:S(2)}) async-start(bf16[64,8,768]{2,1,0:T(8,128)(2,1)} %add_convert_fusion), calls=%async_computation.4 | async-start | bytes 1572864 | tf_op jit(solution)/shard_map/all_to_all | solution.py:121
  142.8 0.2 rev.3
  143.1 23.9 %all-to-all-done.4 = bf16[64,8,768]{2,1,0:T(8,128)(2,1)S(1)} async-done(((bf16[64,8,768]{2,1,0:T(8,128)(2,1)}), bf16[64,8,768]{2,1,0:T(8,128)(2,1)S(1)}, u32[]{:S(2)}, u32[]{:S(2)}) %all-to-all-start.4) | async-done | bytes 786464 | tf_op jit(solution)/shard_map/all_to_all | solution.py:121
  167.2 0.7 fusion.24
  (49 shorter events, 0.8 us)
Async XLA Ops:
  0.6 64.8 %copy-start = (bf16[3,192,768]{2,1,0:T(8,128)(2,1)S(1)}, bf16[3,192,768]{2,1,0:T(8,128)(2,1)}, u32[]{:S(2)}) copy-start(bf16[3,192,768]{2,1,0:T(8,128)(2,1)} %param.13) | copy-start | bytes 2654212
  0.6 18.4 %copy-start.11 = (s32[3,1]{0,1:T(1,128)S(1)}, s32[3,1]{0,1:T(1,128)}, u32[]{:S(2)}) copy-start(s32[3,1]{0,1:T(1,128)} %param.10) | copy-start | bytes 40
  0.7 56.8 %copy-start.2 = (bf16[3,256,768]{2,1,0:T(8,128)(2,1)S(1)}, bf16[3,256,768]{2,1,0:T(8,128)(2,1)}, u32[]{:S(2)}) copy-start(bf16[3,256,768]{2,1,0:T(8,128)(2,1)} %param.12) | copy-start | bytes 3538948
  2.4 40.6 %all-to-all-start = ((bf16[64,8,768]{2,1,0:T(8,128)(2,1)}), bf16[64,8,768]{2,1,0:T(8,128)(2,1)S(1)}, u32[]{:S(2)}, u32[]{:S(2)}) async-start(bf16[64,8,768]{2,1,0:T(8,128)(2,1)} %broadcast_in_dim.101), calls=%async_computation | async-start | bytes 1572864 | tf_op jit(solution)/shard_map/all_to_all | solution.py:14
  19.6 3.1 %collective-permute-start = (s32[1]{0:T(128)}, s32[1]{0:T(128)}, u32[]{:S(2)}, u32[]{:S(2)}) collective-permute-start(s32[1]{0:T(128)} %bitcast.3), channel_id=1, source_target_pairs={{0,4},{4,0},{1,5},{5,1},{2,6},{6,2},{3,7},{7,3},{8,12},{12,8},{9,1... | collective-permute-start | bytes 20 | tf_op jit(solution)/shard_map/ppermute | solution.py:70
  43.0 4.5 %collective-permute-start.1 = (bf16[8,768]{1,0:T(8,128)(2,1)S(1)}, bf16[8,768]{1,0:T(8,128)(2,1)S(1)}, u32[]{:S(2)}, u32[]{:S(2)}) collective-permute-start(bf16[8,768]{1,0:T(8,128)(2,1)S(1)} %get-tuple-element.4), channel_id=1, source_target_pairs={{0,4},{4,0},{1,5},{5,1},{2,6},{6,2},{3,7},{7,3},{8,12},{12,8},{9,1... | collective-permute-start | bytes 36872 | tf_op jit(solution)/shard_map/ppermute | solution.py:72
  60.1 5.1 %copy-start.9 = (s32[3]{0:T(128)S(1)}, s32[3]{0:T(128)}, u32[]{:S(2)}) copy-start(s32[3]{0:T(128)} %param.9) | copy-start | bytes 40
  60.1 59.1 %all-to-all-start.2 = ((bf16[4,3,256,768]{3,2,1,0:T(8,128)(2,1)}), bf16[4,3,256,768]{3,2,1,0:T(8,128)(2,1)}, u32[]{:S(2)}, u32[]{:S(2)}) async-start(bf16[4,3,256,768]{3,2,1,0:T(8,128)(2,1)} %stack.44), calls=%async_computation.2 | async-start | bytes 9437184 | tf_op jit(solution)/shard_map/all_to_all | solution.py:59
  119.2 2.8 %copy-start.10 = (bf16[3,256,1024]{2,1,0:T(8,128)(2,1)S(1)}, bf16[3,256,1024]{2,1,0:T(8,128)(2,1)}, u32[]{:S(2)}) copy-start(bf16[3,256,1024]{2,1,0:T(8,128)(2,1)} %param.11) | copy-start | bytes 4718596
  122.0 1.9 %copy-start.3 = (bf16[3,256,768]{2,1,0:T(8,128)(2,1)S(1)}, bf16[3,256,768]{2,1,0:T(8,128)(2,1)}, u32[]{:S(2)}) copy-start(bf16[3,256,768]{2,1,0:T(8,128)(2,1)} %param.12) | copy-start | bytes 3538948
  123.4 1.0 copy-start.1
  123.9 1.3 copy-start.5
  125.2 9.6 %all-to-all-start.3 = ((bf16[8,2,8,768]{3,2,1,0:T(8,128)(2,1)}), bf16[8,2,8,768]{3,2,1,0:T(8,128)(2,1)S(1)}, u32[]{:S(2)}, u32[]{:S(2)}) async-start(bf16[8,2,8,768]{3,2,1,0:T(8,128)(2,1)} %bitcast.22), calls=%async_computation.3 | async-start | bytes 393216 | tf_op jit(solution)/shard_map/all_to_all | solution.py:106
  128.7 14.1 %copy-start.4 = (bf16[1,8,768]{2,1,0:T(8,128)(2,1)S(1)}, bf16[1,8,768]{2,1,0:T(8,128)(2,1)}, u32[]{:S(2)}) copy-start(bf16[1,8,768]{2,1,0:T(8,128)(2,1)} %param.14) | copy-start | bytes 36868
  134.8 8.2 %copy-start.7 = (f32[1,768]{1,0:T(1,128)S(1)}, f32[1,768]{1,0:T(1,128)}, u32[]{:S(2)}) copy-start(f32[1,768]{1,0:T(1,128)} %param.17) | copy-start | bytes 9220
  134.9 8.2 %copy-start.8 = (f32[1,768]{1,0:T(1,128)S(1)}, f32[1,768]{1,0:T(1,128)}, u32[]{:S(2)}) copy-start(f32[1,768]{1,0:T(1,128)} %param.16) | copy-start | bytes 9220
  134.9 32.2 %copy-start.6 = (f32[1,8,768]{2,1,0:T(8,128)S(1)}, f32[1,8,768]{2,1,0:T(8,128)}, u32[]{:S(2)}) copy-start(f32[1,8,768]{2,1,0:T(8,128)} %param.15) | copy-start | bytes 73732
  136.2 30.8 %all-to-all-start.4 = ((bf16[64,8,768]{2,1,0:T(8,128)(2,1)}), bf16[64,8,768]{2,1,0:T(8,128)(2,1)S(1)}, u32[]{:S(2)}, u32[]{:S(2)}) async-start(bf16[64,8,768]{2,1,0:T(8,128)(2,1)} %add_convert_fusion), calls=%async_computation.4 | async-start | bytes 1572864 | tf_op jit(solution)/shard_map/all_to_all | solution.py:121
